TPU v7x, 128 devices: a whole 4x4x4 slice. The times are simulated.
128 devices in a mesh: ens: 8 (over y, core), trc: 16 (over z, x).
Axes of the slice: x: 4, y: 4, z: 4, core: 2. Of those that a mesh axis runs over, the one named last changes fastest.
Arguments:
- tracer_state: bfloat16 [3072, 4, 16, 1440], P(('ens', 'trc')), may hold values from -6 to 6
- velocity: float32 [2, 4, 16, 1440], replicated, may hold values from -0.24 to 0.24
- land_mask: int32 [16, 1440], replicated, may hold values from 0 to 1, as said below
- in_weight: bfloat16 [24, 256], replicated, may hold values from -1.25 to 1.25
- bias_one: float32 [256], replicated, may hold values from -3 to 3
- hid_weight: bfloat16 [256, 256], replicated, may hold values from -0.375 to 0.375
- bias_two: float32 [256], replicated, may hold values from -3 to 3
- out_coef: float32 [128, 24, 256], P('ens'), may hold values from -6 to 6
- obs_cell: int32 [16, 128], P('trc'), may hold values from 0 to 5759, as said below
- obs_count: int32 [16], P('trc'), may hold values from 16 to 128, as said below
- obs_value: float32 [16, 6, 128], P('trc'), may hold values from -6 to 6
- obs_var: float32 [16, 6, 128], P('trc'), may hold values from 0.05 to 0.5
- obs_noise: float32 [128, 16, 6, 128], P(None, 'trc'), may hold values from -2 to 2
Outputs:
- new_state: bfloat16 [3072, 4, 16, 1440], P('ens', None, 'trc')
- new_coef: float32 [128, 24, 256], P('ens')
Inputs may be any that keep to these rules, and one draw needn't show every extreme that they name: `land_mask`: every block of 1 latitude rows (rows k * 1 to (k + 1) - 1) holds at most 1152 ocean columns, and some block exactly 1152. `obs_cell`: every slot names an ocean cell of its block. `obs_count`: some block uses all 128 slots.
All inputs are finite; a program needn't handle non-finite values.
Results may differ from a plain program's by a relative error of at most 0.0068.
Values may be sent and summed in bfloat16 or wider, within the bound.
No kernel may reach another device: no remote copies, remote signals or barrier semaphores. Data moves between devices by JAX's collectives and lax.ppermute only.
A program may use at most 128 MiB of HBM per device.

v0:
```python
import jax
import jax.numpy as jnp
from jax import lax
from jax.sharding import PartitionSpec as P

OBS_TR = 6
ADV_STEPS = 2
OBS_CAP = 128


def transport(concentration, velocity, sea_mask):
    east_open = sea_mask * jnp.roll(sea_mask, -1, axis=1)
    north_open = sea_mask * jnp.concatenate([sea_mask[1:], jnp.zeros_like(sea_mask[:1])], axis=0)
    east_speed = velocity[0] * east_open
    north_speed = velocity[1] * north_open
    for _ in range(ADV_STEPS):
        east_value = jnp.roll(concentration, -1, axis=-1)
        east_flux = (
            jnp.maximum(east_speed, 0.0) * concentration + jnp.minimum(east_speed, 0.0) * east_value
        )
        north_value = jnp.concatenate(
            [concentration[..., 1:, :], jnp.zeros_like(concentration[..., :1, :])], axis=-2
        )
        north_flux = (
            jnp.maximum(north_speed, 0.0) * concentration
            + jnp.minimum(north_speed, 0.0) * north_value
        )
        west_flux = jnp.roll(east_flux, 1, axis=-1)
        south_flux = jnp.concatenate(
            [jnp.zeros_like(north_flux[..., :1, :]), north_flux[..., :-1, :]], axis=-2
        )
        concentration = concentration - (east_flux - west_flux) - (north_flux - south_flux)
    return concentration


def silu(value):
    return value * (0.5 + 0.5 * jnp.tanh(0.5 * value))


def tree_sum(value, axis_name, size):
    if size & size - 1:
        return lax.psum(value, axis_name)
    step = 1
    while step < size:
        pairs = [(i, i ^ step) for i in range(size)]
        value = value + lax.ppermute(value, axis_name, pairs)
        step *= 2
    return value


def reaction(fields, in_weight, bias_one, hid_weight, bias_two, member_coef, sea_cells):
    contract = (((0,), (0,)), ((), ()))
    hidden_one = lax.dot_general(in_weight, fields, contract, preferred_element_type=jnp.float32)
    hidden_one = silu(hidden_one + bias_one[:, None]).astype(jnp.bfloat16)
    hidden_two = lax.dot_general(
        hid_weight, hidden_one, contract, preferred_element_type=jnp.float32
    )
    hidden_two = silu(hidden_two + bias_two[:, None]).astype(jnp.bfloat16)
    tendency = jnp.dot(
        member_coef, hidden_two, preferred_element_type=jnp.float32
    ) * hid_weight.shape[0] ** (-0.5)
    return ((fields.astype(jnp.float32) + tendency) * sea_cells).astype(jnp.bfloat16)


def solve_system(system, right_side):
    factor = jnp.linalg.cholesky(system)
    middle = lax.linalg.triangular_solve(factor, right_side, left_side=True, lower=True)
    return lax.linalg.triangular_solve(factor, middle, left_side=True, lower=True, transpose_a=True)


def shards(
    tracer_state,
    velocity,
    land_mask,
    in_weight,
    bias_one,
    hid_weight,
    bias_two,
    out_coef,
    obs_cell,
    obs_count,
    obs_value,
    obs_var,
    obs_noise,
):
    blocks = lax.axis_size("trc")
    own_block = lax.axis_index("trc")
    group_index = lax.axis_index("ens")
    field_rows, levels, lat_rows, lon_count = tracer_state.shape
    row_block = lat_rows // blocks
    block_width = row_block * lon_count
    members_here = out_coef.shape[0]
    tracers = in_weight.shape[0]
    group_rows = members_here * tracers
    highest = lax.Precision.HIGHEST
    sea_mask = land_mask.astype(jnp.float32)
    coef_all = lax.all_gather(out_coef.reshape(out_coef.shape[0], -1), "ens", axis=0, tiled=True)
    advected = transport(tracer_state.astype(jnp.float32) * sea_mask, velocity, sea_mask).astype(
        jnp.bfloat16
    )
    coef_half = out_coef.astype(jnp.bfloat16)
    sea_own = lax.dynamic_slice_in_dim(sea_mask, own_block * row_block, row_block, 0)
    gathered = lax.all_to_all(advected, "trc", split_axis=2, concat_axis=0, tiled=True)
    out_shape = gathered.shape
    grouped = gathered.reshape(members_here, tracers, -1)
    sea_cells = jnp.broadcast_to(sea_own[None], (out_shape[1],) + sea_own.shape).reshape(-1)

    def one_member(inputs):
        fields, member_coef = inputs
        return reaction(fields, in_weight, bias_one, hid_weight, bias_two, member_coef, sea_cells)

    reacted = lax.map(one_member, (grouped, coef_half))
    new_cols = reacted.reshape(out_shape)
    new_flat = new_cols.reshape(group_rows, levels, block_width)
    observed = new_flat.reshape(members_here, tracers, levels * block_width)[:, :OBS_TR]
    observed = observed.reshape(members_here * OBS_TR, levels * block_width)
    cell_ids = lax.broadcasted_iota(jnp.int32, (levels * block_width, OBS_CAP), 0)
    picker = (cell_ids == obs_cell[0][None, :]).astype(jnp.bfloat16)
    picked = jnp.dot(observed, picker, preferred_element_type=jnp.float32)
    predicted_own = picked.astype(jnp.bfloat16).reshape(members_here, OBS_TR, OBS_CAP)
    predicted_all = lax.all_gather(predicted_own, "ens", axis=0, tiled=True)
    member_total = predicted_all.shape[0]
    slot_ids = jnp.arange(OBS_CAP, dtype=jnp.int32)
    valid_slots = (slot_ids < obs_count[0]).astype(jnp.float32)
    weight = valid_slots[None, :] / obs_var[0]
    guessed = predicted_all.astype(jnp.float32).reshape(member_total, -1)
    anomaly = guessed - jnp.mean(guessed, axis=0)
    misfit = (obs_value[None] + obs_noise).reshape(member_total, -1) - guessed
    weighted = anomaly * weight.reshape(1, -1)
    gram_part = jnp.dot(weighted, anomaly.T, precision=highest, preferred_element_type=jnp.float32)
    cross_part = jnp.dot(weighted, misfit.T, precision=highest, preferred_element_type=jnp.float32)
    both = tree_sum(jnp.stack([gram_part, cross_part]), "trc", blocks)
    gram, cross = (both[0], both[1])
    system = (member_total - 1) * jnp.eye(member_total, dtype=jnp.float32) + gram
    mixing = solve_system(system, cross)
    flat_coef = out_coef.reshape(members_here, -1)
    first_member = group_index * members_here
    mixing_cols = lax.dynamic_slice_in_dim(mixing, first_member, members_here, 1)
    summed = jnp.dot(mixing_cols.T, coef_all, precision=highest, preferred_element_type=jnp.float32)
    new_coef = flat_coef + summed
    return (new_cols, new_coef.reshape(members_here, tracers, -1))


def solution(mesh):
    in_specs = (
        P(("ens", "trc"), None, None, None),
        P(),
        P(),
        P(),
        P(),
        P(),
        P(),
        P("ens", None, None),
        P("trc", None),
        P("trc"),
        P("trc", None, None),
        P("trc", None, None),
        P(None, "trc", None, None),
    )
    out_specs = (P("ens", None, "trc", None), P("ens", None, None))
    return jax.shard_map(shards, mesh=mesh, in_specs=in_specs, out_specs=out_specs, check_vma=False)
```

profile of v0, /device:TPU:6, one launch (start us, length us, event | category | flops | bytes accessed | tf_op | source)
XLA Modules:
  0.0 444.6 jit_solution(4422173835736729489)
XLA Ops:
  8.2 5.3 %convert_multiply_fusion = f32[24,4,16,1440]{3,0,1,2:T(8,128)S(1)} fusion(f32[16,1440]{1,0:T(8,128)S(1)} %convert_element_type.40, bf16[24,4,16,1440]{3,2,1,0:T(8,128)(2,1)} %param.15), kind=kLoop, calls=%fused_computation.34 | loop fusion | flops 4423680 | bytes 13363200 | tf_op jit(solution)/shard_map/mul | solution.py:98
  13.4 6.1 %slice.102 = f32[24,4,16,1439]{3,0,1,2:T(8,128)} slice(f32[24,4,16,1440]{3,0,1,2:T(8,128)S(1)} %convert_multiply_fusion), slice={[0:24], [0:4], [0:16], [1:1440]} | slice | bytes 17682432 | tf_op jit(solution)/shard_map/jit(_roll_static)/slice | solution.py:17
  26.1 13.3 %multiply_add_fusion.1 = (f32[24,4,16,1440]{3,0,1,2:T(8,128)S(1)}, f32[24,4,16,1440]{3,0,1,2:T(8,128)S(1)}) fusion(f32[24,4,15,1440]{3,0,1,2:T(8,128)} %slice.107, f32[4,16,1440]{2,0,1:T(4,128)S(1)} %copy.69, f32[4,16,1440]{2,0,1:T(4,128)S(1)} %copy.68, f32[16,1440]{1,0:T(8,128)S(1)} %convert_element_type.40, bf16[24,4,16,1440]{3,2,1,0:T(8,128)(2,1)} %param.15, ...), kind=kLoop, calls=%fused_computation.33 | loop fusion | flops 19906560 | bytes 40826880 | tf_op jit(solution)/shard_map/add | solution.py:25
  39.4 4.8 %slice.108 = f32[24,4,15,1440]{3,0,1,2:T(8,128)} slice(f32[24,4,16,1440]{3,0,1,2:T(8,128)S(1)} %get-tuple-element.101), slice={[0:24], [0:4], [0:15], [0:1440]} | slice | bytes 16588800 | tf_op jit(solution)/shard_map/slice | solution.py:30
  48.7 15.4 %fusion.18 = f32[24,4,16,1440]{3,0,1,2:T(8,128)S(1)} fusion(f32[24,4,16,1440]{3,0,1,2:T(8,128)} %copy-done, f32[24,4,16,1439]{3,0,1,2:T(8,128)} %bitcast.104, f32[24,4,16,1]{3,0,1,2:T(8,128)} %slice.104, f32[24,4,16,1440]{3,0,1,2:T(8,128)} %copy-done.1, f32[24,4,15,1440]{3,0,1,2:T(8,128)} %slice.108, f32[16,1440]{1,0:T(8,128)S(1)} %convert_element_type.40, ...), kind=kLoop, calls=%fused_computation.25 | loop fusion | flops 15482880 | bytes 48199680 | tf_op jit(solution)/shard_map/sub | solution.py:32
  64.1 6.2 %slice.109 = f32[24,4,16,1439]{3,0,1,2:T(8,128)} slice(f32[24,4,16,1440]{3,0,1,2:T(8,128)S(1)} %fusion.18), slice={[0:24], [0:4], [0:16], [1:1440]} | slice | bytes 17682432 | tf_op jit(solution)/shard_map/jit(_roll_static)/slice | solution.py:17
  74.7 17.6 %multiply_add_fusion = (f32[24,4,16,1440]{3,0,1,2:T(8,128)}, f32[24,4,16,1440]{3,0,1,2:T(8,128)}) fusion(f32[24,4,15,1440]{3,0,1,2:T(8,128)} %slice.113, f32[24,4,16,1440]{3,0,1,2:T(8,128)S(1)} %fusion.18, f32[4,16,1440]{2,0,1:T(4,128)S(1)} %copy.69, f32[4,16,1440]{2,0,1:T(4,128)S(1)} %copy.68, f32[24,4,16,1]{3,0,1,2:T(8,128)S(1)} %slice.110, ...), kind=kLoop, calls=%fused_computation.32 | loop fusion | flops 15482880 | bytes 45158400 | tf_op jit(solution)/shard_map/add | solution.py:25
  92.3 8.2 %slice.114 = f32[24,4,15,1440]{3,0,1,2:T(8,128)} slice(f32[24,4,16,1440]{3,0,1,2:T(8,128)} %get-tuple-element.99), slice={[0:24], [0:4], [0:15], [0:1440]} | slice | bytes 16588800 | tf_op jit(solution)/shard_map/slice | solution.py:30
  101.9 16.1 %fusion.22 = bf16[24,4,16,1440]{3,0,1,2:T(8,128)(2,1)} fusion(f32[24,4,16,1440]{3,0,1,2:T(8,128)S(1)} %fusion.18, f32[24,4,16,1440]{3,0,1,2:T(8,128)} %get-tuple-element.100, f32[24,4,16,1439]{3,0,1,2:T(8,128)} %bitcast.103, f32[24,4,16,1]{3,0,1,2:T(8,128)S(1)} %slice.111, f32[24,4,16,1440]{3,0,1,2:T(8,128)} %get-tuple-element.99, f32[24,4,15,1440]{3,0,1,2:T(8,128)} %slice.114), kind=kLoop, calls=%fused_computation.31 | loop fusion | flops 13271040 | bytes 48107520 | tf_op jit(solution)/shard_map/convert_element_type | solution.py:98
  118.0 8.4 %all-to-all-start = ((bf16[24,4,16,1440]{3,0,1,2:T(8,128)(2,1)}), bf16[24,4,16,1440]{3,0,1,2:T(8,128)(2,1)}, u32[]{:S(2)}, u32[]{:S(2)}) async-start(bf16[24,4,16,1440]{3,0,1,2:T(8,128)(2,1)} %fusion.22), calls=%async_computation | async-start | bytes 9437184 | tf_op jit(solution)/shard_map/all_to_all | solution.py:103
  128.2 67.1 %all-to-all-done = bf16[24,4,16,1440]{3,0,1,2:T(8,128)(2,1)} async-done(((bf16[24,4,16,1440]{3,0,1,2:T(8,128)(2,1)}), bf16[24,4,16,1440]{3,0,1,2:T(8,128)(2,1)}, u32[]{:S(2)}, u32[]{:S(2)}) %all-to-all-start) | async-done | bytes 4423712 | tf_op jit(solution)/shard_map/all_to_all | solution.py:103
  195.3 7.0 %copy.70 = bf16[16,24,4,1,1440]{4,2,1,0,3:T(4,128)(2,1)} copy(bf16[16,24,4,1,1440]{4,1,2,0,3:T(8,128)(2,1)} %bitcast.5) | data formatting | bytes 8847360 | tf_op jit(solution)/shard_map/all_to_all | solution.py:103
  202.3 8.6 %reshape.103 = bf16[16,24,5760]{2,1,0:T(8,128)(2,1)} reshape(bf16[16,24,4,1,1440]{4,2,1,0,3:T(4,128)(2,1)} %copy.70) | data formatting | bytes 8847360 | tf_op jit(solution)/shard_map/reshape | solution.py:105
  210.9 138.9 %while.11 = (s32[]{:T(128)}, bf16[16,24,5760]{2,1,0:T(8,128)(2,1)}, bf16[16,24,5760]{2,1,0:T(8,128)(2,1)}, bf16[16,24,256]{2,1,0:T(8,128)(2,1)S(1)}, bf16[24,256...) while((s32[]{:T(128)}, bf16[16,24,5760]{2,1,0:T(8,128)(2,1)}, ...), condition=%wide.region_1.2_spmd.clone, body=%wide.region_0.1_spmd.clone.sunk | while | flops 914918400 | bytes 6986469 | solution.py:112
  215.3 4.4 fusion.59
  224.0 4.4 fusion.59
  232.7 4.4 fusion.59
  241.3 4.4 fusion.59
  250.0 4.4 fusion.59
  258.7 4.4 fusion.59
  267.4 4.4 fusion.59
  276.0 4.4 fusion.59
  284.7 4.4 fusion.59
  302.1 4.4 fusion.59
  352.6 13.5 %all_gather.6 = bf16[128,6,128]{2,0,1:T(8,128)(2,1)S(1)} all-gather(bf16[16,6,128]{2,0,1:T(8,128)(2,1)S(1)} %copy.71), channel_id=1, replica_groups=mesh['ens'=8,'trc'=16] {'ens'}, dimensions={0}, use_global_device_ids=true | all-gather | bytes 221184 | tf_op jit(solution)/shard_map/all_gather | solution.py:121
  369.2 5.7 %collective-permute-done = f32[2,128,128]{2,1,0:T(8,128)S(1)} collective-permute-done((f32[2,128,128]{2,1,0:T(8,128)S(1)}, f32[2,128,128]{2,1,0:T(8,128)S(1)}, u32[]{:S(2)}, u32[]{:S(2)}) %collective-permute-start) | collective-permute-done | bytes 131104 | tf_op jit(solution)/shard_map/ppermute | solution.py:46
  376.8 4.7 %collective-permute-done.1 = f32[2,128,128]{2,1,0:T(8,128)S(1)} collective-permute-done((f32[2,128,128]{2,1,0:T(8,128)S(1)}, f32[2,128,128]{2,1,0:T(8,128)S(1)}, u32[]{:S(2)}, u32[]{:S(2)}) %collective-permute-start.1) | collective-permute-done | bytes 131104 | tf_op jit(solution)/shard_map/ppermute | solution.py:46
  382.1 4.5 %collective-permute-done.2 = f32[2,128,128]{2,1,0:T(8,128)S(1)} collective-permute-done((f32[2,128,128]{2,1,0:T(8,128)S(1)}, f32[2,128,128]{2,1,0:T(8,128)S(1)}, u32[]{:S(2)}, u32[]{:S(2)}) %collective-permute-start.2) | collective-permute-done | bytes 131104 | tf_op jit(solution)/shard_map/ppermute | solution.py:46
  390.2 10.5 %reshape.104 = bf16[384,4,1,1440]{3,1,0,2:T(4,128)(2,1)} reshape(bf16[16,24,5760]{2,1,0:T(8,128)(2,1)} %get-tuple-element.49) | data formatting | bytes 8847360 | tf_op jit(solution)/shard_map/reshape | solution.py:113
  400.7 8.8 %copy.79 = bf16[384,4,1,1440]{0,3,2,1:T(8,128)(2,1)} copy(bf16[384,4,1,1440]{3,1,0,2:T(4,128)(2,1)} %reshape.104) | data formatting | bytes 8847360
  409.7 11.7 %cholesky.16 = f32[128,128]{1,0:T(8,128)S(1)} custom-call(f32[128,128]{1,0:T(8,128)S(1)} %fusion.35), custom_call_target="Cholesky" | custom-call | tf_op jit(solution)/shard_map/jit(cholesky)/cholesky | solution.py:66
  422.7 9.8 %custom-call.8 = f32[1,128,128]{1,2,0:T(8,128)S(1)} custom-call(f32[1,128,128]{2,1,0:T(8,128)S(1)} %fusion.29), custom_call_target="InvertDiagBlocksLowerTriangular" | custom-call | tf_op jit(solution)/shard_map/triangular_solve | solution.py:68
  (142 shorter events, 132.1 us)
Async XLA Ops:
  19.6 5.2 %copy-start.6 = (s32[16,1440]{1,0:T(8,128)S(1)}, s32[16,1440]{1,0:T(8,128)}, u32[]{:S(2)}) copy-start(s32[16,1440]{1,0:T(8,128)} %param.17) | copy-start | bytes 276484
  19.6 5.3 %copy-start.4 = (f32[2,4,16,1440]{3,2,1,0:T(8,128)S(1)}, f32[2,4,16,1440]{3,2,1,0:T(8,128)}, u32[]{:S(2)}) copy-start(f32[2,4,16,1440]{3,2,1,0:T(8,128)} %param.16) | copy-start | bytes 2211844
  39.4 7.2 %copy-start = (f32[24,4,16,1440]{3,0,1,2:T(8,128)}, f32[24,4,16,1440]{3,0,1,2:T(8,128)S(1)}, u32[]{:S(2)}) copy-start(f32[24,4,16,1440]{3,0,1,2:T(8,128)S(1)} %get-tuple-element.102) | copy-start | bytes 26542084
  39.4 9.3 %copy-start.1 = (f32[24,4,16,1440]{3,0,1,2:T(8,128)}, f32[24,4,16,1440]{3,0,1,2:T(8,128)S(1)}, u32[]{:S(2)}) copy-start(f32[24,4,16,1440]{3,0,1,2:T(8,128)S(1)} %get-tuple-element.101) | copy-start | bytes 26542084
  118.0 8.5 %copy-start.3 = (f32[16,24,256]{2,1,0:T(8,128)S(1)}, f32[16,24,256]{2,1,0:T(8,128)}, u32[]{:S(2)}) copy-start(f32[16,24,256]{2,1,0:T(8,128)} %param.22) | copy-start | bytes 1179652
  118.0 10.2 %copy-start.7 = (f32[1,6,128]{2,0,1:T(1,128)S(1)}, f32[1,6,128]{2,0,1:T(1,128)}, u32[]{:S(2)}) copy-start(f32[1,6,128]{2,0,1:T(1,128)} %param.25) | copy-start | bytes 9220
  118.0 10.2 %copy-start.8 = (f32[1,6,128]{2,0,1:T(1,128)S(1)}, f32[1,6,128]{2,0,1:T(1,128)}, u32[]{:S(2)}) copy-start(f32[1,6,128]{2,0,1:T(1,128)} %param.26) | copy-start | bytes 9220
  118.0 77.3 %all-to-all-start = ((bf16[24,4,16,1440]{3,0,1,2:T(8,128)(2,1)}), bf16[24,4,16,1440]{3,0,1,2:T(8,128)(2,1)}, u32[]{:S(2)}, u32[]{:S(2)}) async-start(bf16[24,4,16,1440]{3,0,1,2:T(8,128)(2,1)} %fusion.22), calls=%async_computation | async-start | bytes 9437184 | tf_op jit(solution)/shard_map/all_to_all | solution.py:103
  126.4 306.7 %all-gather.2.cloned.1.call-start = ((), (), s32[]{:S(2)}) async-start(), calls=%async_computation.1 | async-start | bytes 3538944 | tf_op jit(solution)/shard_map/all_gather | solution.py:97
  127.4 83.5 %copy-start.9 = (bf16[256,256]{1,0:T(8,128)(2,1)S(1)}, bf16[256,256]{1,0:T(8,128)(2,1)}, u32[]{:S(2)}) copy-start(bf16[256,256]{1,0:T(8,128)(2,1)} %param.20) | copy-start | bytes 393220
  127.4 83.5 %copy-start.10 = (bf16[24,256]{1,0:T(8,128)(2,1)S(1)}, bf16[24,256]{1,0:T(8,128)(2,1)}, u32[]{:S(2)}) copy-start(bf16[24,256]{1,0:T(8,128)(2,1)} %param.18) | copy-start | bytes 36868
  127.4 83.5 %copy-start.11 = (f32[256]{0:T(256)S(1)}, f32[256]{0:T(256)}, u32[]{:S(2)}) copy-start(f32[256]{0:T(256)} %param.19) | copy-start | bytes 3076
  127.4 83.5 %copy-start.12 = (f32[256]{0:T(256)S(1)}, f32[256]{0:T(256)}, u32[]{:S(2)}) copy-start(f32[256]{0:T(256)} %param.21) | copy-start | bytes 3076
  210.9 140.9 %copy-start.13 = (s32[1,128]{1,0:T(1,128)S(1)}, s32[1,128]{1,0:T(1,128)}, u32[]{:S(2)}) copy-start(s32[1,128]{1,0:T(1,128)} %param.23) | copy-start | bytes 1540
  210.9 155.5 %copy-start.5 = (f32[128,1,6,128]{3,1,2,0:T(1,128)S(1)}, f32[128,1,6,128]{3,1,2,0:T(1,128)}, u32[]{:S(2)}) copy-start(f32[128,1,6,128]{3,1,2,0:T(1,128)} %param.27) | copy-start | bytes 1179652
  369.1 5.8 %collective-permute-start = (f32[2,128,128]{2,1,0:T(8,128)S(1)}, f32[2,128,128]{2,1,0:T(8,128)S(1)}, u32[]{:S(2)}, u32[]{:S(2)}) collective-permute-start(f32[2,128,128]{2,1,0:T(8,128)S(1)} %pad_maximum_fusion), channel_id=1, source_target_pairs={{0,1},{1,0},{2,3},{3,2},{4,5},{5,4},{6,7},{7,6},{8,9},{9,8},{10,11... | collective-permute-start | bytes 393224 | tf_op jit(solution)/shard_map/ppermute | solution.py:46
  375.0 6.6 %collective-permute-start.1 = (f32[2,128,128]{2,1,0:T(8,128)S(1)}, f32[2,128,128]{2,1,0:T(8,128)S(1)}, u32[]{:S(2)}, u32[]{:S(2)}) collective-permute-start(f32[2,128,128]{2,1,0:T(8,128)S(1)} %fusion.38), channel_id=1, source_target_pairs={{0,2},{1,3},{2,0},{3,1},{4,6},{5,7},{6,4},{7,5},{8,10},{9,11},{10,... | collective-permute-start | bytes 393224 | tf_op jit(solution)/shard_map/ppermute | solution.py:46
  381.5 5.0 %collective-permute-start.2 = (f32[2,128,128]{2,1,0:T(8,128)S(1)}, f32[2,128,128]{2,1,0:T(8,128)S(1)}, u32[]{:S(2)}, u32[]{:S(2)}) collective-permute-start(f32[2,128,128]{2,1,0:T(8,128)S(1)} %fusion.47), channel_id=1, source_target_pairs={{0,4},{1,5},{2,6},{3,7},{4,0},{5,1},{6,2},{7,3},{8,12},{9,13},{10,... | collective-permute-start | bytes 393224 | tf_op jit(solution)/shard_map/ppermute | solution.py:46
  386.6 22.9 %collective-permute-start.3 = (f32[2,128,128]{2,1,0:T(8,128)S(1)}, f32[2,128,128]{2,1,0:T(8,128)S(1)}, u32[]{:S(2)}, u32[]{:S(2)}) collective-permute-start(f32[2,128,128]{2,1,0:T(8,128)S(1)} %add.113), channel_id=1, source_target_pairs={{0,8},{1,9},{2,10},{3,11},{4,12},{5,13},{6,14},{7,15},{8,0},{9,1},... | collective-permute-start | bytes 393224 | tf_op jit(solution)/shard_map/ppermute | solution.py:46
  390.2 42.9 %copy-start.2 = (f32[2,8,24,256]{3,1,2,0:T(8,128)S(1)}, f32[2,8,24,256]{3,1,2,0:T(8,128)}, u32[]{:S(2)}) copy-start(f32[2,8,24,256]{3,1,2,0:T(8,128)} %copy.84) | copy-start | bytes 1179652
Sparse Core Ops, SparseCore 0:
  129.4 28.9 all-gather.1
where the time goes:
time: 452 us; the launch traced here: 445 us
  matrix products  144 us (32%)
  other arithmetic  92.1 us (20%)
  local copies, waits for them, and re-layouts  83.2 us (18%)
  waiting for transfers between devices  82.1 us (18%)
  between operations  15.4 us (3%)
  starting transfers between devices  14.5 us (3%)
  blocking collectives  13.5 us (3%)
    dot_general x16, matrix products, reaction(): jnp.dot(member_coef, hidden_two, preferred_element_type=jnp.float32)  70 us
    all_to_all x1, waiting for transfers between devices, shards(): lax.all_to_all(advected, 'trc', split_axis=2, concat_axis=0, tiled=True)  67.1 us
    dot_general x16, matrix products, reaction(): lax.dot_general(in_weight, fields, contract, preferred_element_type=jnp.f...  66.8 us
    add x2, other arithmetic, transport(): jnp.maximum(north_speed, 0.0) * concentration  30.8 us
    convert_element_type x1, other arithmetic, shards(): transport(tracer_state.astype(jnp.float32) * sea_mask, velocity, sea_mask)  16.1 us
    sub x1, other arithmetic, transport(): concentration - (east_flux - west_flux) - (north_flux - south_flux)  15.4 us
    ppermute x4, waiting for transfers between devices, tree_sum(): value = value + lax.ppermute(value, axis_name, pairs)  15 us
    all_gather x1, blocking collectives, shards(): predicted_all = lax.all_gather(predicted_own, 'ens', axis=0, tiled=True)  13.5 us
  transfers between devices with their start and end apart: 6, of which 4 were waited for; matrix products, arithmetic and copies ran while one was open for 46% of the time, Pallas kernels for 0%

commit v1 on v0

--- a/solution.py
+++ b/solution.py
@@ -6,6 +6,12 @@
 OBS_TR = 6
 ADV_STEPS = 2
 OBS_CAP = 128
+
+
+def tiled_gather(x, axis, dim):
+    size = lax.axis_size(axis)
+    repeats = [size if d == dim else 1 for d in range(x.ndim)]
+    return lax.all_to_all(jnp.tile(x, repeats), axis, split_axis=dim, concat_axis=dim, tiled=True)
 
 
 def transport(concentration, velocity, sea_mask):
@@ -118,7 +124,7 @@
     picker = (cell_ids == obs_cell[0][None, :]).astype(jnp.bfloat16)
     picked = jnp.dot(observed, picker, preferred_element_type=jnp.float32)
     predicted_own = picked.astype(jnp.bfloat16).reshape(members_here, OBS_TR, OBS_CAP)
-    predicted_all = lax.all_gather(predicted_own, "ens", axis=0, tiled=True)
+    predicted_all = tiled_gather(predicted_own, "ens", 0)
     member_total = predicted_all.shape[0]
     slot_ids = jnp.arange(OBS_CAP, dtype=jnp.int32)
     valid_slots = (slot_ids < obs_count[0]).astype(jnp.float32)

time: 452 us -> 452 us (level)
  blocking collectives: 13.5 us -> 0 us
  waiting for transfers between devices: 82.1 us -> 89.5 us
    all_gather x1 -> x0, blocking collectives: 13.5 us -> none  [shards(): predicted_all = lax.all_gather(predicted_own, 'ens', axis=0, tiled=True)]
    all_to_all x0 -> x1, waiting for transfers between devices: none -> 7.44 us  [tiled_gather(): lax.all_to_all(jnp.tile(x, repeats), axis, split_axis=dim, concat_axis=di...]
    all_to_all x0 -> x1, starting transfers between devices: none -> 4.71 us  [tiled_gather(): lax.all_to_all(jnp.tile(x, repeats), axis, split_axis=dim, concat_axis=di...]
  transfers between devices with their start and end apart: 6 -> 7, of which waited for: 4 -> 5; matrix products, arithmetic and copies ran while one was open for 46% -> 46% of each run, Pallas kernels for 0% -> 0%
where the time goes in v1:
time: 452 us; the launch traced here: 444 us
  matrix products  144 us (32%)
  other arithmetic  92.2 us (20%)
  waiting for transfers between devices  89.5 us (20%)
  local copies, waits for them, and re-layouts  84.2 us (19%)
  starting transfers between devices  19 us (4%)
  between operations  15.4 us (3%)
    dot_general x16, matrix products, reaction(): jnp.dot(member_coef, hidden_two, preferred_element_type=jnp.float32)  70 us
    all_to_all x1, waiting for transfers between devices, shards(): lax.all_to_all(advected, 'trc', split_axis=2, concat_axis=0, tiled=True)  67.1 us
    dot_general x16, matrix products, reaction(): lax.dot_general(in_weight, fields, contract, preferred_element_type=jnp.f...  66.9 us
    add x2, other arithmetic, transport(): jnp.maximum(north_speed, 0.0) * concentration  30.8 us
    convert_element_type x1, other arithmetic, shards(): transport(tracer_state.astype(jnp.float32) * sea_mask, velocity, sea_mask)  16 us
    sub x1, other arithmetic, transport(): concentration - (east_flux - west_flux) - (north_flux - south_flux)  15.4 us
    ppermute x4, waiting for transfers between devices, tree_sum(): value = value + lax.ppermute(value, axis_name, pairs)  14.9 us
    slice x4, local copies, waits for them, and re-layouts, transport(): east_value = jnp.roll(concentration, -1, axis=-1)  13.4 us
  transfers between devices with their start and end apart: 7, of which 5 were waited for; matrix products, arithmetic and copies ran while one was open for 46% of the time, Pallas kernels for 0%

profile of v1, /device:TPU:6, one launch (start us, length us, event | category | flops | bytes accessed | tf_op | source)
XLA Modules:
  0.0 444.2 jit_solution(7806094792333127996)
XLA Ops:
  8.2 5.3 %convert_multiply_fusion = f32[24,4,16,1440]{3,0,1,2:T(8,128)S(1)} fusion(f32[16,1440]{1,0:T(8,128)S(1)} %convert_element_type.40, bf16[24,4,16,1440]{3,2,1,0:T(8,128)(2,1)} %param.15), kind=kLoop, calls=%fused_computation.34 | loop fusion | flops 4423680 | bytes 13363200 | tf_op jit(solution)/shard_map/mul | solution.py:104
  13.4 6.2 %slice.102 = f32[24,4,16,1439]{3,0,1,2:T(8,128)} slice(f32[24,4,16,1440]{3,0,1,2:T(8,128)S(1)} %convert_multiply_fusion), slice={[0:24], [0:4], [0:16], [1:1440]} | slice | bytes 17682432 | tf_op jit(solution)/shard_map/jit(_roll_static)/slice | solution.py:23
  26.2 13.3 %multiply_add_fusion.1 = (f32[24,4,16,1440]{3,0,1,2:T(8,128)S(1)}, f32[24,4,16,1440]{3,0,1,2:T(8,128)S(1)}) fusion(f32[24,4,15,1440]{3,0,1,2:T(8,128)} %slice.107, f32[4,16,1440]{2,0,1:T(4,128)S(1)} %copy.69, f32[4,16,1440]{2,0,1:T(4,128)S(1)} %copy.68, f32[16,1440]{1,0:T(8,128)S(1)} %convert_element_type.40, bf16[24,4,16,1440]{3,2,1,0:T(8,128)(2,1)} %param.15, ...), kind=kLoop, calls=%fused_computation.33 | loop fusion | flops 19906560 | bytes 40826880 | tf_op jit(solution)/shard_map/add | solution.py:31
  39.4 4.8 %slice.108 = f32[24,4,15,1440]{3,0,1,2:T(8,128)} slice(f32[24,4,16,1440]{3,0,1,2:T(8,128)S(1)} %get-tuple-element.101), slice={[0:24], [0:4], [0:15], [0:1440]} | slice | bytes 16588800 | tf_op jit(solution)/shard_map/slice | solution.py:36
  48.8 15.4 %fusion.18 = f32[24,4,16,1440]{3,0,1,2:T(8,128)S(1)} fusion(f32[24,4,16,1440]{3,0,1,2:T(8,128)} %copy-done, f32[24,4,16,1439]{3,0,1,2:T(8,128)} %bitcast.105, f32[24,4,16,1]{3,0,1,2:T(8,128)} %slice.104, f32[24,4,16,1440]{3,0,1,2:T(8,128)} %copy-done.1, f32[24,4,15,1440]{3,0,1,2:T(8,128)} %slice.108, f32[16,1440]{1,0:T(8,128)S(1)} %convert_element_type.40, ...), kind=kLoop, calls=%fused_computation.25 | loop fusion | flops 15482880 | bytes 48199680 | tf_op jit(solution)/shard_map/sub | solution.py:38
  64.1 6.2 %slice.109 = f32[24,4,16,1439]{3,0,1,2:T(8,128)} slice(f32[24,4,16,1440]{3,0,1,2:T(8,128)S(1)} %fusion.18), slice={[0:24], [0:4], [0:16], [1:1440]} | slice | bytes 17682432 | tf_op jit(solution)/shard_map/jit(_roll_static)/slice | solution.py:23
  74.7 17.6 %multiply_add_fusion = (f32[24,4,16,1440]{3,0,1,2:T(8,128)}, f32[24,4,16,1440]{3,0,1,2:T(8,128)}) fusion(f32[24,4,15,1440]{3,0,1,2:T(8,128)} %slice.113, f32[24,4,16,1440]{3,0,1,2:T(8,128)S(1)} %fusion.18, f32[4,16,1440]{2,0,1:T(4,128)S(1)} %copy.69, f32[4,16,1440]{2,0,1:T(4,128)S(1)} %copy.68, f32[24,4,16,1]{3,0,1,2:T(8,128)S(1)} %slice.110, ...), kind=kLoop, calls=%fused_computation.32 | loop fusion | flops 15482880 | bytes 45158400 | tf_op jit(solution)/shard_map/add | solution.py:31
  92.3 8.2 %slice.114 = f32[24,4,15,1440]{3,0,1,2:T(8,128)} slice(f32[24,4,16,1440]{3,0,1,2:T(8,128)} %get-tuple-element.99), slice={[0:24], [0:4], [0:15], [0:1440]} | slice | bytes 16588800 | tf_op jit(solution)/shard_map/slice | solution.py:36
  102.0 16.0 %fusion.22 = bf16[24,4,16,1440]{3,0,1,2:T(8,128)(2,1)} fusion(f32[24,4,16,1440]{3,0,1,2:T(8,128)S(1)} %fusion.18, f32[24,4,16,1440]{3,0,1,2:T(8,128)} %get-tuple-element.100, f32[24,4,16,1439]{3,0,1,2:T(8,128)} %bitcast.104, f32[24,4,16,1]{3,0,1,2:T(8,128)S(1)} %slice.111, f32[24,4,16,1440]{3,0,1,2:T(8,128)} %get-tuple-element.99, f32[24,4,15,1440]{3,0,1,2:T(8,128)} %slice.114), kind=kLoop, calls=%fused_computation.31 | loop fusion | flops 13271040 | bytes 48107520 | tf_op jit(solution)/shard_map/convert_element_type | solution.py:104
  118.0 8.4 %all-to-all-start = ((bf16[24,4,16,1440]{3,0,1,2:T(8,128)(2,1)}), bf16[24,4,16,1440]{3,0,1,2:T(8,128)(2,1)}, u32[]{:S(2)}, u32[]{:S(2)}) async-start(bf16[24,4,16,1440]{3,0,1,2:T(8,128)(2,1)} %fusion.22), calls=%async_computation | async-start | bytes 9437184 | tf_op jit(solution)/shard_map/all_to_all | solution.py:109
  128.2 67.1 %all-to-all-done = bf16[24,4,16,1440]{3,0,1,2:T(8,128)(2,1)} async-done(((bf16[24,4,16,1440]{3,0,1,2:T(8,128)(2,1)}), bf16[24,4,16,1440]{3,0,1,2:T(8,128)(2,1)}, u32[]{:S(2)}, u32[]{:S(2)}) %all-to-all-start) | async-done | bytes 4423712 | tf_op jit(solution)/shard_map/all_to_all | solution.py:109
  195.3 6.9 %copy.70 = bf16[16,24,4,1,1440]{4,2,1,0,3:T(4,128)(2,1)} copy(bf16[16,24,4,1,1440]{4,1,2,0,3:T(8,128)(2,1)} %bitcast.5) | data formatting | bytes 8847360 | tf_op jit(solution)/shard_map/all_to_all | solution.py:109
  202.3 8.6 %reshape.104 = bf16[16,24,5760]{2,1,0:T(8,128)(2,1)} reshape(bf16[16,24,4,1,1440]{4,2,1,0,3:T(4,128)(2,1)} %copy.70) | data formatting | bytes 8847360 | tf_op jit(solution)/shard_map/reshape | solution.py:111
  210.9 139.0 %while.11 = (s32[]{:T(128)}, bf16[16,24,5760]{2,1,0:T(8,128)(2,1)}, bf16[16,24,5760]{2,1,0:T(8,128)(2,1)}, bf16[16,24,256]{2,1,0:T(8,128)(2,1)S(1)}, bf16[24,256...) while((s32[]{:T(128)}, bf16[16,24,5760]{2,1,0:T(8,128)(2,1)}, ...), condition=%wide.region_1.2_spmd.clone, body=%wide.region_0.1_spmd.clone.sunk | while | flops 914918400 | bytes 6986469 | solution.py:118
  215.3 4.4 fusion.59
  224.0 4.4 fusion.59
  241.3 4.4 fusion.59
  258.7 4.4 fusion.59
  276.1 4.4 fusion.59
  293.4 4.4 fusion.59
  310.8 4.4 fusion.59
  328.2 4.4 fusion.59
  345.6 4.4 fusion.59
  353.7 4.7 %all-to-all-start.1 = ((bf16[128,6,128]{2,1,0:T(8,128)(2,1)}), bf16[128,6,128]{2,1,0:T(8,128)(2,1)S(1)}, u32[]{:S(2)}, u32[]{:S(2)}) async-start(bf16[128,6,128]{2,1,0:T(8,128)(2,1)} %copy.72), calls=%async_computation.1 | async-start | bytes 524288 | tf_op jit(solution)/shard_map/all_to_all | solution.py:14
  358.4 7.4 %all-to-all-done.1 = bf16[128,6,128]{2,1,0:T(8,128)(2,1)S(1)} async-done(((bf16[128,6,128]{2,1,0:T(8,128)(2,1)}), bf16[128,6,128]{2,1,0:T(8,128)(2,1)S(1)}, u32[]{:S(2)}, u32[]{:S(2)}) %all-to-all-start.1) | async-done | bytes 196640 | tf_op jit(solution)/shard_map/all_to_all | solution.py:14
  369.0 5.0 %collective-permute-done = f32[2,128,128]{2,1,0:T(8,128)S(1)} collective-permute-done((f32[2,128,128]{2,1,0:T(8,128)S(1)}, f32[2,128,128]{2,1,0:T(8,128)S(1)}, u32[]{:S(2)}, u32[]{:S(2)}) %collective-permute-start) | collective-permute-done | bytes 131104 | tf_op jit(solution)/shard_map/ppermute | solution.py:52
  375.7 4.8 %collective-permute-done.1 = f32[2,128,128]{2,1,0:T(8,128)S(1)} collective-permute-done((f32[2,128,128]{2,1,0:T(8,128)S(1)}, f32[2,128,128]{2,1,0:T(8,128)S(1)}, u32[]{:S(2)}, u32[]{:S(2)}) %collective-permute-start.1) | collective-permute-done | bytes 131104 | tf_op jit(solution)/shard_map/ppermute | solution.py:52
  381.0 5.1 %collective-permute-done.2 = f32[2,128,128]{2,1,0:T(8,128)S(1)} collective-permute-done((f32[2,128,128]{2,1,0:T(8,128)S(1)}, f32[2,128,128]{2,1,0:T(8,128)S(1)}, u32[]{:S(2)}, u32[]{:S(2)}) %collective-permute-start.2) | collective-permute-done | bytes 131104 | tf_op jit(solution)/shard_map/ppermute | solution.py:52
  389.7 10.5 %reshape.105 = bf16[384,4,1,1440]{3,1,0,2:T(4,128)(2,1)} reshape(bf16[16,24,5760]{2,1,0:T(8,128)(2,1)} %get-tuple-element.49) | data formatting | bytes 8847360 | tf_op jit(solution)/shard_map/reshape | solution.py:119
  400.2 8.8 %copy.80 = bf16[384,4,1,1440]{0,3,2,1:T(8,128)(2,1)} copy(bf16[384,4,1,1440]{3,1,0,2:T(4,128)(2,1)} %reshape.105) | data formatting | bytes 8847360
  409.2 11.7 %cholesky.16 = f32[128,128]{1,0:T(8,128)S(1)} custom-call(f32[128,128]{1,0:T(8,128)S(1)} %fusion.35), custom_call_target="Cholesky" | custom-call | tf_op jit(solution)/shard_map/jit(cholesky)/cholesky | solution.py:72
  422.3 9.8 %custom-call.8 = f32[1,128,128]{1,2,0:T(8,128)S(1)} custom-call(f32[1,128,128]{2,1,0:T(8,128)S(1)} %fusion.29), custom_call_target="InvertDiagBlocksLowerTriangular" | custom-call | tf_op jit(solution)/shard_map/triangular_solve | solution.py:74
  (145 shorter events, 137.4 us)
Async XLA Ops:
  19.6 5.2 %copy-start.6 = (s32[16,1440]{1,0:T(8,128)S(1)}, s32[16,1440]{1,0:T(8,128)}, u32[]{:S(2)}) copy-start(s32[16,1440]{1,0:T(8,128)} %param.17) | copy-start | bytes 276484
  19.6 5.3 %copy-start.4 = (f32[2,4,16,1440]{3,2,1,0:T(8,128)S(1)}, f32[2,4,16,1440]{3,2,1,0:T(8,128)}, u32[]{:S(2)}) copy-start(f32[2,4,16,1440]{3,2,1,0:T(8,128)} %param.16) | copy-start | bytes 2211844
  39.4 7.2 %copy-start = (f32[24,4,16,1440]{3,0,1,2:T(8,128)}, f32[24,4,16,1440]{3,0,1,2:T(8,128)S(1)}, u32[]{:S(2)}) copy-start(f32[24,4,16,1440]{3,0,1,2:T(8,128)S(1)} %get-tuple-element.102) | copy-start | bytes 26542084
  39.4 9.3 %copy-start.1 = (f32[24,4,16,1440]{3,0,1,2:T(8,128)}, f32[24,4,16,1440]{3,0,1,2:T(8,128)S(1)}, u32[]{:S(2)}) copy-start(f32[24,4,16,1440]{3,0,1,2:T(8,128)S(1)} %get-tuple-element.101) | copy-start | bytes 26542084
  118.0 8.5 %copy-start.3 = (f32[16,24,256]{2,1,0:T(8,128)S(1)}, f32[16,24,256]{2,1,0:T(8,128)}, u32[]{:S(2)}) copy-start(f32[16,24,256]{2,1,0:T(8,128)} %param.22) | copy-start | bytes 1179652
  118.0 10.2 %copy-start.7 = (f32[1,6,128]{2,0,1:T(1,128)S(1)}, f32[1,6,128]{2,0,1:T(1,128)}, u32[]{:S(2)}) copy-start(f32[1,6,128]{2,0,1:T(1,128)} %param.25) | copy-start | bytes 9220
  118.0 77.3 %all-to-all-start = ((bf16[24,4,16,1440]{3,0,1,2:T(8,128)(2,1)}), bf16[24,4,16,1440]{3,0,1,2:T(8,128)(2,1)}, u32[]{:S(2)}, u32[]{:S(2)}) async-start(bf16[24,4,16,1440]{3,0,1,2:T(8,128)(2,1)} %fusion.22), calls=%async_computation | async-start | bytes 9437184 | tf_op jit(solution)/shard_map/all_to_all | solution.py:109
  126.4 306.4 %all-gather.2.cloned.1.call-start = ((), (), s32[]{:S(2)}) async-start(), calls=%async_computation.2 | async-start | bytes 3538944 | tf_op jit(solution)/shard_map/all_gather | solution.py:103
  127.4 83.5 %copy-start.9 = (bf16[256,256]{1,0:T(8,128)(2,1)S(1)}, bf16[256,256]{1,0:T(8,128)(2,1)}, u32[]{:S(2)}) copy-start(bf16[256,256]{1,0:T(8,128)(2,1)} %param.20) | copy-start | bytes 393220
  127.4 83.5 %copy-start.10 = (bf16[24,256]{1,0:T(8,128)(2,1)S(1)}, bf16[24,256]{1,0:T(8,128)(2,1)}, u32[]{:S(2)}) copy-start(bf16[24,256]{1,0:T(8,128)(2,1)} %param.18) | copy-start | bytes 36868
  127.4 83.5 %copy-start.11 = (f32[256]{0:T(256)S(1)}, f32[256]{0:T(256)}, u32[]{:S(2)}) copy-start(f32[256]{0:T(256)} %param.19) | copy-start | bytes 3076
  127.4 83.5 %copy-start.12 = (f32[256]{0:T(256)S(1)}, f32[256]{0:T(256)}, u32[]{:S(2)}) copy-start(f32[256]{0:T(256)} %param.21) | copy-start | bytes 3076
  210.9 141.0 %copy-start.13 = (s32[1,128]{1,0:T(1,128)S(1)}, s32[1,128]{1,0:T(1,128)}, u32[]{:S(2)}) copy-start(s32[1,128]{1,0:T(1,128)} %param.23) | copy-start | bytes 1540
  210.9 147.4 %copy-start.8 = (f32[1,6,128]{2,0,1:T(1,128)S(1)}, f32[1,6,128]{2,0,1:T(1,128)}, u32[]{:S(2)}) copy-start(f32[1,6,128]{2,0,1:T(1,128)} %param.26) | copy-start | bytes 9220
  349.9 16.3 %copy-start.5 = (f32[128,1,6,128]{3,1,2,0:T(1,128)S(1)}, f32[128,1,6,128]{3,1,2,0:T(1,128)}, u32[]{:S(2)}) copy-start(f32[128,1,6,128]{3,1,2,0:T(1,128)} %param.27) | copy-start | bytes 1179652
  353.7 12.2 %all-to-all-start.1 = ((bf16[128,6,128]{2,1,0:T(8,128)(2,1)}), bf16[128,6,128]{2,1,0:T(8,128)(2,1)S(1)}, u32[]{:S(2)}, u32[]{:S(2)}) async-start(bf16[128,6,128]{2,1,0:T(8,128)(2,1)} %copy.72), calls=%async_computation.1 | async-start | bytes 524288 | tf_op jit(solution)/shard_map/all_to_all | solution.py:14
  368.9 5.0 %collective-permute-start = (f32[2,128,128]{2,1,0:T(8,128)S(1)}, f32[2,128,128]{2,1,0:T(8,128)S(1)}, u32[]{:S(2)}, u32[]{:S(2)}) collective-permute-start(f32[2,128,128]{2,1,0:T(8,128)S(1)} %pad_maximum_fusion), channel_id=1, source_target_pairs={{0,1},{1,0},{2,3},{3,2},{4,5},{5,4},{6,7},{7,6},{8,9},{9,8},{10,11... | collective-permute-start | bytes 393224 | tf_op jit(solution)/shard_map/ppermute | solution.py:52
  373.9 6.6 %collective-permute-start.1 = (f32[2,128,128]{2,1,0:T(8,128)S(1)}, f32[2,128,128]{2,1,0:T(8,128)S(1)}, u32[]{:S(2)}, u32[]{:S(2)}) collective-permute-start(f32[2,128,128]{2,1,0:T(8,128)S(1)} %fusion.38), channel_id=1, source_target_pairs={{0,2},{1,3},{2,0},{3,1},{4,6},{5,7},{6,4},{7,5},{8,10},{9,11},{10,... | collective-permute-start | bytes 393224 | tf_op jit(solution)/shard_map/ppermute | solution.py:52
  380.5 5.6 %collective-permute-start.2 = (f32[2,128,128]{2,1,0:T(8,128)S(1)}, f32[2,128,128]{2,1,0:T(8,128)S(1)}, u32[]{:S(2)}, u32[]{:S(2)}) collective-permute-start(f32[2,128,128]{2,1,0:T(8,128)S(1)} %fusion.47), channel_id=1, source_target_pairs={{0,4},{1,5},{2,6},{3,7},{4,0},{5,1},{6,2},{7,3},{8,12},{9,13},{10,... | collective-permute-start | bytes 393224 | tf_op jit(solution)/shard_map/ppermute | solution.py:52
  386.2 22.9 %collective-permute-start.3 = (f32[2,128,128]{2,1,0:T(8,128)S(1)}, f32[2,128,128]{2,1,0:T(8,128)S(1)}, u32[]{:S(2)}, u32[]{:S(2)}) collective-permute-start(f32[2,128,128]{2,1,0:T(8,128)S(1)} %add.113), channel_id=1, source_target_pairs={{0,8},{1,9},{2,10},{3,11},{4,12},{5,13},{6,14},{7,15},{8,0},{9,1},... | collective-permute-start | bytes 393224 | tf_op jit(solution)/shard_map/ppermute | solution.py:52
  389.7 43.0 %copy-start.2 = (f32[2,8,24,256]{3,1,2,0:T(8,128)S(1)}, f32[2,8,24,256]{3,1,2,0:T(8,128)}, u32[]{:S(2)}) copy-start(f32[2,8,24,256]{3,1,2,0:T(8,128)} %copy.85) | copy-start | bytes 1179652
Sparse Core Ops, SparseCore 0:
  129.5 28.9 all-gather.1
